TPU v7x, 32 devices: a whole 2x2x4 slice. The times are simulated.
32 devices in a mesh: group: 2 (over x), dev: 16 (over z, y, core).
Axes of the slice: x: 2, y: 2, z: 4, core: 2. Of those that a mesh axis runs over, the one named last changes fastest.
Arguments:
- suffix_x: bfloat16 [2, 4096, 1600], P('group', 'dev'), may hold values from -6 to 6
- suffix_query: bfloat16 [2, 4096, 1024], P('group', 'dev'), may hold values from -128 to 128
- suffix_keyval: bfloat16 [2, 4096, 2048], P('group', 'dev'), may hold values from -6 to 6
- prefix_keyval: bfloat16 [2, 128, 2048], P('group', 'dev'), may hold values from -6 to 6
- prefix_hidden: bfloat16 [2, 128, 1600], P('group', 'dev'), may hold values from -6 to 6
- kv_weight: bfloat16 [1600, 2048], replicated, may hold values from -0.15625 to 0.15625
- out_weight: bfloat16 [1024, 1600], replicated, may hold values from -0.1875 to 0.1875
- fc_weight: bfloat16 [1600, 3840], P(None, ('group', 'dev')), may hold values from -0.15625 to 0.15625
- proj_weight: bfloat16 [3840, 1600], P(('group', 'dev')), may hold values from -0.09375 to 0.09375
- lengths: int32 [2, 16], P('group'), may hold values from 1 to 256, 2048 in all within a row
- placement: int32 [2, 16], P('group'), may hold values from 0 to 15, each once within a row
- owners: int32 [2, 16], P('group'), may hold values from 0 to 15, each once within a row
- recompute: int32 [2, 2], P('group'), may hold values from 0 to 15
Outputs:
- layer_out: bfloat16 [2, 4096, 1600], P('group', 'dev')
All inputs are finite; a program needn't handle non-finite values.
Results may differ from a plain program's by a relative error of at most 0.008.
Values may be sent and summed in bfloat16 or wider, within the bound.
No kernel may reach another device: no remote copies, remote signals or barrier semaphores. Data moves between devices by JAX's collectives and lax.ppermute only.
A program may use at most 128 MiB of HBM per device.

v0:
```python
import jax
import jax.numpy as jnp
from jax import lax
from jax.sharding import PartitionSpec as P

HEAD_DIM = 64
NEGATIVE = -1e30
EPSILON = 1e-05
SCORE_SCALE = 0.125


def normalize(values_in):
    values_in = values_in.astype(jnp.float32)
    average = jnp.mean(values_in, axis=-1, keepdims=True)
    centered = values_in - average
    variance = jnp.mean(centered * centered, axis=-1, keepdims=True)
    return centered / jnp.sqrt(variance + EPSILON)


def absorb(state, queries, keyval, allowed):
    running_top, running_total, accumulated = state
    head_count = queries.shape[1]
    head_size = queries.shape[2]
    row_count = keyval.shape[0]
    width_att = head_count * head_size
    key_rows = keyval[:, :width_att].reshape(row_count, head_count, head_size)
    val_rows = keyval[:, width_att:].reshape(row_count, head_count, head_size)
    scores = (
        jnp.einsum("qhd,khd->hqk", queries, key_rows, preferred_element_type=jnp.float32)
        * SCORE_SCALE
    )
    scores = jnp.where(allowed[None], scores, NEGATIVE)
    new_top = jnp.maximum(running_top, jnp.max(scores, axis=-1))
    factor = jnp.exp(running_top - new_top)
    weights = jnp.where(allowed[None], jnp.exp(scores - new_top[:, :, None]), 0.0)
    running_total = running_total * factor + jnp.sum(weights, axis=-1)
    weights_low = weights.astype(jnp.bfloat16)
    update = jnp.einsum("hqk,khd->qhd", weights_low, val_rows, preferred_element_type=jnp.float32)
    accumulated = accumulated * jnp.transpose(factor)[:, :, None] + update
    return (new_top, running_total, accumulated)


def per_device(
    suffix_x,
    suffix_query,
    suffix_keyval,
    prefix_keyval,
    prefix_hidden,
    kv_weight,
    out_weight,
    fc_weight,
    proj_weight,
    lengths,
    placement,
    owners,
    recompute,
):
    device_count = lax.axis_size("dev")
    my_device = lax.axis_index("dev")
    slots = suffix_x.shape[1]
    block_rows = prefix_keyval.shape[1]
    width_att = suffix_query.shape[2]
    head_count = width_att // HEAD_DIM
    device_ids = jnp.arange(device_count, dtype=jnp.int32)
    hits = placement[0][:, None] == device_ids[None, :]
    device_length = jnp.sum(jnp.where(hits, lengths[0][:, None], 0), axis=0)
    my_length = jnp.sum(jnp.where(device_ids == my_device, device_length, 0))
    block_ids = jnp.arange(owners.shape[1], dtype=jnp.int32)
    chosen = recompute[0]
    chosen_owner = jnp.sum(
        jnp.where(chosen[:, None] == block_ids[None, :], owners[0][None, :], 0), axis=1
    )
    stale_device = jnp.any(chosen_owner[:, None] == device_ids[None, :], axis=0)
    queries = suffix_query[0].reshape(slots, head_count, HEAD_DIM)
    normed_prefix = normalize(prefix_hidden[0]).astype(jnp.bfloat16)
    fresh = jnp.dot(normed_prefix, kv_weight, preferred_element_type=jnp.float32).astype(
        jnp.bfloat16
    )
    my_stale = jnp.any(chosen_owner == my_device)
    local_kv = jnp.where(my_stale, fresh, prefix_keyval[0])
    skip_device = jnp.zeros_like(stale_device)
    gathered = lax.all_gather(local_kv, "dev", axis=0, tiled=True)
    prefix_count = gathered.shape[0]
    row_device = jnp.arange(prefix_count, dtype=jnp.int32) // block_rows
    skipped = jnp.any((row_device[:, None] == device_ids[None, :]) & skip_device[None, :], axis=1)
    state = (
        jnp.full((head_count, slots), NEGATIVE, jnp.float32),
        jnp.zeros((head_count, slots), jnp.float32),
        jnp.zeros((slots, head_count, HEAD_DIM), jnp.float32),
    )
    key_block = 512 if prefix_count % 512 == 0 else prefix_count
    for block_start in range(0, prefix_count, key_block):
        kept = jnp.logical_not(skipped[block_start : block_start + key_block])
        allowed = jnp.broadcast_to(kept[None, :], (slots, key_block))
        state = absorb(state, queries, gathered[block_start : block_start + key_block], allowed)
    positions = jnp.arange(slots, dtype=jnp.int32)
    causal = (positions[None, :] <= positions[:, None]) & (positions[None, :] < my_length)
    state = absorb(state, queries, suffix_keyval[0], causal)
    final_top, final_total, accumulated = state
    attended = (
        (accumulated / jnp.transpose(final_total)[:, :, None])
        .reshape(slots, width_att)
        .astype(jnp.bfloat16)
    )
    projected = jnp.dot(attended, out_weight, preferred_element_type=jnp.float32)
    residual = suffix_x[0].astype(jnp.float32) + projected
    normed = normalize(residual).astype(jnp.bfloat16)
    fc_full, proj_full = (
        lax.all_gather(fc_weight, ("group", "dev"), axis=1, tiled=True),
        lax.all_gather(proj_weight, ("group", "dev"), axis=0, tiled=True),
    )
    inner = jnp.dot(normed, fc_full, preferred_element_type=jnp.float32)
    activated = jax.nn.gelu(inner, approximate=True).astype(jnp.bfloat16)
    feed_out = jnp.dot(activated, proj_full, preferred_element_type=jnp.float32)
    live = positions[:, None] < my_length
    return jnp.where(live, residual + feed_out, 0.0).astype(jnp.bfloat16)[None]


def solution(mesh):
    return jax.shard_map(
        per_device,
        mesh=mesh,
        in_specs=(
            P("group", "dev", None),
            P("group", "dev", None),
            P("group", "dev", None),
            P("group", "dev", None),
            P("group", "dev", None),
            P(),
            P(),
            P(None, ("group", "dev")),
            P(("group", "dev"), None),
            P("group", None),
            P("group", None),
            P("group", None),
            P("group", None),
        ),
        out_specs=P("group", "dev", None),
        check_vma=False,
    )
```

profile of v0, /device:TPU:0, one launch (start us, length us, event | category | flops | bytes accessed | tf_op | source)
XLA Modules:
  0.0 235.2 jit_solution(8602153443183435182)
XLA Ops:
  6.5 0.0 copy-start
  6.5 0.0 all-gather.3.cloned.1.call-start
  6.6 0.7 all-gather.3.cloned.1.call-update
  7.3 0.0 all-gather.5.cloned.1.call-start
  7.3 0.7 all-gather.5.cloned.1.call-update
  8.0 2.2 fusion.67
  10.3 2.0 copy.33
  12.3 2.1 copy.30
  14.4 0.0 copy-done.8
  14.4 0.0 copy-done.7
  14.4 0.2 fusion.55
  14.6 0.6 compare_reduce_fusion
  15.2 0.0 copy-done.4
  15.2 0.1 convert_reduce_fusion
  15.4 0.2 fusion.46
  15.6 0.0 copy-done.5
  15.6 0.0 copy-start.9
  15.6 0.0 copy-start.10
  15.6 4.5 %fusion.14 = bf16[8,2048]{1,0:T(8,128)(2,1)S(1)} fusion(bf16[1600,2048]{1,0:T(8,128)(2,1)} %param.18, bf16[1,8,2048]{2,1,0:T(8,128)(2,1)S(1)} %copy-done.5, pred[]{:T(512)} %compare_reduce_fusion, bf16[1,8,1600]{2,1,0:T(8,128)(2,1)S(1)} %copy-done.4, f32[8]{0:T(128)S(1)} %add_sqrt_fusion.1, f32[8]{0:T(128)S(1)} %broadcast_multiply_fusion.1), kind=kOutput, calls=%fused_computation.20 | convolution fusion | flops 52512768 | bytes 6644801 | tf_op jit(solution)/shard_map/dot_general | solution.py:76
  20.1 25.2 %all_gather.9 = bf16[128,2048]{1,0:T(8,128)(2,1)S(1)} all-gather(bf16[8,2048]{1,0:T(8,128)(2,1)S(1)} %fusion.14), channel_id=1, replica_groups=mesh['group'=2,'dev'=16] {'dev'}, dimensions={0}, use_global_device_ids=true | all-gather | bytes 557056 | tf_op jit(solution)/shard_map/all_gather | solution.py:82
  45.3 0.7 fusion.68
  46.1 1.8 copy.29
  47.9 2.0 copy.34
  49.9 0.8 copy.31
  50.7 0.0 copy-done.9
  50.8 0.0 copy-done.10
  50.8 0.1 select_reduce_fusion
  50.8 0.6 fusion.56
  51.5 0.6 iota_compare_fusion.2
  52.1 0.1 fusion.42
  52.2 1.6 bitcast_reduce_fusion
  53.9 2.0 fusion.8
  55.9 0.0 copy-start.2
  55.9 0.4 fusion.24
  56.3 1.0 fusion.9
  57.3 0.0 copy-done.2
  57.3 0.0 copy-start.3
  57.3 1.1 fusion.26
  58.5 0.0 copy-done.3
  58.5 0.6 fusion.33
  59.1 0.0 copy-done
  59.1 0.5 copy-done.6
  59.6 1.1 fusion.69
  60.7 1.2 copy-done.1
  61.9 0.2 multiply_reduce_fusion
  62.2 49.0 %all-gather.3.cloned.1.call-done = bf16[1600,3840]{0,1:T(8,128)(2,1)} async-done(((bf16[1600,120]{0,1:T(8,128)(2,1)}), bf16[1600,3840]{0,1:T(8,128)(2,1)}) %all-gather.3.cloned.1.call-update) | async-done | bytes 12288016 | tf_op jit(solution)/shard_map/all_gather | solution.py:109
  111.2 98.2 %all-gather.5.cloned.1.call-done = bf16[3840,1600]{1,0:T(8,128)(2,1)} async-done(((bf16[120,1600]{1,0:T(8,128)(2,1)}), bf16[3840,1600]{1,0:T(8,128)(2,1)}) %all-gather.5.cloned.1.call-update) | async-done | bytes 12288016 | tf_op jit(solution)/shard_map/all_gather | solution.py:110
  209.4 19.0 %fusion.13 = bf16[1,256,1600]{1,2,0:T(8,128)(2,1)} fusion(f32[256,1600]{0,1:T(8,128)} %copy-done.1, bf16[3840,1600]{1,0:T(8,128)(2,1)} %all-gather.5.cloned.1.call-done, bf16[1600,3840]{0,1:T(8,128)(2,1)} %all-gather.3.cloned.1.call-done, f32[256]{0:T(256)S(1)} %add_sqrt_fusion, f32[256]{0:T(256)S(1)} %broadcast_multiply_fusion, ...), kind=kOutput, calls=%fused_computation.18 | convolution fusion | flops 6302760960 | bytes 27035904 | tf_op jit(solution)/shard_map/dot_general | solution.py:114
  (12 shorter events, 0.1 us)
Async XLA Ops:
  6.5 52.6 %copy-start = (bf16[1024,1600]{0,1:T(8,128)(2,1)S(1)}, bf16[1024,1600]{0,1:T(8,128)(2,1)}, u32[]{:S(2)}) copy-start(bf16[1024,1600]{0,1:T(8,128)(2,1)} %param.19) | copy-start | bytes 9830404
  6.5 7.9 %copy-start.8 = (s32[1,2]{1,0:T(1,128)S(1)}, s32[1,2]{1,0:T(1,128)}, u32[]{:S(2)}) copy-start(s32[1,2]{1,0:T(1,128)} %param.25) | copy-start | bytes 28
  6.5 7.9 %copy-start.7 = (s32[1,16]{1,0:T(1,128)S(1)}, s32[1,16]{1,0:T(1,128)}, u32[]{:S(2)}) copy-start(s32[1,16]{1,0:T(1,128)} %param.24) | copy-start | bytes 196
  6.5 8.7 %copy-start.4 = (bf16[1,8,1600]{2,1,0:T(8,128)(2,1)S(1)}, bf16[1,8,1600]{2,1,0:T(8,128)(2,1)}, u32[]{:S(2)}) copy-start(bf16[1,8,1600]{2,1,0:T(8,128)(2,1)} %param.17) | copy-start | bytes 76804
  6.5 9.1 %copy-start.5 = (bf16[1,8,2048]{2,1,0:T(8,128)(2,1)S(1)}, bf16[1,8,2048]{2,1,0:T(8,128)(2,1)}, u32[]{:S(2)}) copy-start(bf16[1,8,2048]{2,1,0:T(8,128)(2,1)} %param.16) | copy-start | bytes 98308
  6.5 104.7 %all-gather.3.cloned.1.call-start = ((), (), s32[]{:S(2)}) async-start(), calls=%async_computation | async-start | bytes 13178880 | tf_op jit(solution)/shard_map/all_gather | solution.py:109
  7.3 202.1 %all-gather.5.cloned.1.call-start = ((), (), s32[]{:S(2)}) async-start(), calls=%async_computation.1 | async-start | bytes 13178880 | tf_op jit(solution)/shard_map/all_gather | solution.py:110
  15.6 35.2 %copy-start.9 = (s32[1,16]{1,0:T(1,128)S(1)}, s32[1,16]{1,0:T(1,128)}, u32[]{:S(2)}) copy-start(s32[1,16]{1,0:T(1,128)} %param.22) | copy-start | bytes 196
  15.6 35.1 %copy-start.10 = (s32[1,16]{1,0:T(1,128)S(1)}, s32[1,16]{1,0:T(1,128)}, u32[]{:S(2)}) copy-start(s32[1,16]{1,0:T(1,128)} %param.23) | copy-start | bytes 196
  55.9 1.4 copy-start.2
  57.3 1.1 copy-start.3
  58.5 1.2 copy-start.6
  60.7 1.2 copy-start.1
Sparse Core Ops, SparseCore 0:
  10.2 100.9 all-gather.2
  114.0 95.2 all-gather.4
where the time goes:
time: 236 us; the launch traced here: 235 us
  waiting for transfers between devices  149 us (63%)
  matrix products  29.9 us (13%)
  blocking collectives  25.2 us (11%)
  local copies, waits for them, and re-layouts  13.6 us (6%)
  between operations  13.6 us (6%)
  other arithmetic  4.28 us (2%)
    all_gather x1, waiting for transfers between devices, per_device(): lax.all_gather(proj_weight, ('group', 'dev'), axis=0, tiled=True)  98.2 us
    all_gather x1, waiting for transfers between devices, per_device(): lax.all_gather(fc_weight, ('group', 'dev'), axis=1, tiled=True)  49 us
    all_gather x1, blocking collectives, per_device(): gathered = lax.all_gather(local_kv, 'dev', axis=0, tiled=True)  25.2 us
    dot_general x1, matrix products, per_device(): feed_out = jnp.dot(activated, proj_full, preferred_element_type=jnp.float32)  19 us
    slice x3, local copies, waits for them, and re-layouts, absorb(): key_rows = keyval[:, :width_att].reshape(row_count, head_count, head_size)  6.07 us
  transfers between devices with their start and end apart: 2, of which 2 were waited for; matrix products, arithmetic and copies ran while one was open for 11% of the time, Pallas kernels for 0%

commit v1 on v0

--- a/solution.py
+++ b/solution.py
@@ -7,6 +7,30 @@
 NEGATIVE = -1e30
 EPSILON = 1e-05
 SCORE_SCALE = 0.125
+
+
+def _step_on_terms(v0, dim_no):
+    arr_next = list(v0.shape[1:])
+    arr_next[dim_no] *= v0.shape[0]
+    r2 = jnp.moveaxis(v0, 0, dim_no).reshape(arr_next)
+    return r2
+
+
+def shape_counts_on_mesh(own_rows, chip_axis):
+    n = jax.lax.psum(1, chip_axis)
+    formed = own_rows[None]
+    for c in range(n.bit_length() - 1):
+        outer = 1 << c
+        mid_arr = jax.lax.ppermute(formed, chip_axis, [(i, i ^ outer) for i in range(n)])
+        s_next = jnp.stack([formed, mid_arr], axis=0)
+        mat_out = jax.lax.axis_index(chip_axis) >> c & 1
+        formed = jnp.where(mat_out == 0, s_next, s_next[::-1]).reshape(-1, *own_rows.shape)
+    return formed
+
+
+def watch_the_signs(field_in, q_in, ndim_at):
+    reached = _step_on_terms(shape_counts_on_mesh(q_in, field_in), ndim_at)
+    return reached
 
 
 def normalize(values_in):
@@ -107,7 +131,7 @@
     normed = normalize(residual).astype(jnp.bfloat16)
     fc_full, proj_full = (
         lax.all_gather(fc_weight, ("group", "dev"), axis=1, tiled=True),
-        lax.all_gather(proj_weight, ("group", "dev"), axis=0, tiled=True),
+        watch_the_signs(("group", "dev"), proj_weight, 0),
     )
     inner = jnp.dot(normed, fc_full, preferred_element_type=jnp.float32)
     activated = jax.nn.gelu(inner, approximate=True).astype(jnp.bfloat16)

time: 236 us -> 449 us (1.90)
  waiting for transfers between devices: 149 us -> 327 us
  other arithmetic: 4.28 us -> 34.5 us
  starting transfers between devices: 0.08 us -> 11.1 us
    ppermute x0 -> x5, waiting for transfers between devices: none -> 326 us  [shape_counts_on_mesh(): jax.lax.ppermute(formed, chip_axis, [(i, i ^ outer) for i in range(n)])]
    all_gather x1 -> x0, waiting for transfers between devices: 98.2 us -> none  [per_device(): lax.all_gather(proj_weight, ('group', 'dev'), axis=0, tiled=True)]
    all_gather x1, waiting for transfers between devices: 49 us -> 0.01 us  [per_device(): lax.all_gather(fc_weight, ('group', 'dev'), axis=1, tiled=True)]
    another operation x0 -> x6, other arithmetic: none -> 16.3 us  [shape_counts_on_mesh(): s_next = jnp.stack([formed, mid_arr], axis=0)]
    select_n x0 -> x4, other arithmetic: none -> 14 us  [shape_counts_on_mesh(): jnp.where(mat_out == 0, s_next, s_next[::-1]).reshape(-1, *own_rows.shape)]
    ppermute x0 -> x5, starting transfers between devices: none -> 11.1 us  [shape_counts_on_mesh(): jax.lax.ppermute(formed, chip_axis, [(i, i ^ outer) for i in range(n)])]
  transfers between devices with their start and end apart: 2 -> 6, of which waited for: 2 -> 5; matrix products, arithmetic and copies ran while one was open for 11% -> 13% of each run, Pallas kernels for 0% -> 0%
where the time goes in v1:
time: 449 us; the launch traced here: 448 us
  waiting for transfers between devices  327 us (73%)
  other arithmetic  34.5 us (8%)
  matrix products  30 us (7%)
  blocking collectives  21 us (5%)
  between operations  13.6 us (3%)
  local copies, waits for them, and re-layouts  11.2 us (2%)
  starting transfers between devices  11.1 us (2%)
    ppermute x5, waiting for transfers between devices, shape_counts_on_mesh(): jax.lax.ppermute(formed, chip_axis, [(i, i ^ outer) for i in range(n)])  326 us
    all_gather x1, blocking collectives, per_device(): gathered = lax.all_gather(local_kv, 'dev', axis=0, tiled=True)  21 us
    dot_general x1, matrix products, per_device(): feed_out = jnp.dot(activated, proj_full, preferred_element_type=jnp.float32)  19 us
    another operation x6, other arithmetic, shape_counts_on_mesh(): s_next = jnp.stack([formed, mid_arr], axis=0)  16.3 us
    select_n x4, other arithmetic, shape_counts_on_mesh(): jnp.where(mat_out == 0, s_next, s_next[::-1]).reshape(-1, *own_rows.shape)  14 us
    ppermute x5, starting transfers between devices, shape_counts_on_mesh(): jax.lax.ppermute(formed, chip_axis, [(i, i ^ outer) for i in range(n)])  11.1 us
  transfers between devices with their start and end apart: 6, of which 5 were waited for; matrix products, arithmetic and copies ran while one was open for 13% of the time, Pallas kernels for 0%

profile of v1, /device:TPU:0, one launch (start us, length us, event | category | flops | bytes accessed | tf_op | source)
XLA Modules:
  0.0 448.3 jit_solution(13098763553106306503)
XLA Ops:
  6.5 0.7 all-gather.2.cloned.1.call-update
  7.3 0.5 collective-permute-start
  7.8 1.7 collective-permute-done
  9.5 1.2 pad_maximum_fusion.4
  10.7 1.4 fusion.43
  12.1 2.9 collective-permute-start.1
  15.0 21.2 %collective-permute-done.1 = bf16[2,120,1600]{2,1,0:T(8,128)(2,1)} collective-permute-done((bf16[2,120,1600]{2,1,0:T(8,128)(2,1)}, bf16[2,120,1600]{2,1,0:T(8,128)(2,1)}, u32[]{:S(2)}, u32[]{:S(2)}) %collective-permute-start.1) | collective-permute-done | bytes 768032 | tf_op jit(solution)/shard_map/ppermute | solution.py:24
  36.2 1.6 pad_maximum_fusion.3
  37.8 1.5 reverse_select_fusion.3
  39.2 1.8 collective-permute-start.2
  41.0 69.7 %collective-permute-done.2 = bf16[4,120,1600]{2,1,0:T(8,128)(2,1)} collective-permute-done((bf16[4,120,1600]{2,1,0:T(8,128)(2,1)}, bf16[4,120,1600]{2,1,0:T(8,128)(2,1)}, u32[]{:S(2)}, u32[]{:S(2)}) %collective-permute-start.2) | collective-permute-done | bytes 1536032 | tf_op jit(solution)/shard_map/ppermute | solution.py:24
  110.7 2.2 pad_maximum_fusion.2
  112.9 2.3 reverse_select_fusion.2
  115.2 4.3 collective-permute-start.3
  119.5 144.0 %collective-permute-done.3 = bf16[8,120,1600]{2,1,0:T(8,128)(2,1)} collective-permute-done((bf16[8,120,1600]{2,1,0:T(8,128)(2,1)}, bf16[8,120,1600]{2,1,0:T(8,128)(2,1)}, u32[]{:S(2)}, u32[]{:S(2)}) %collective-permute-start.3) | collective-permute-done | bytes 3072032 | tf_op jit(solution)/shard_map/ppermute | solution.py:24
  263.5 3.6 pad_maximum_fusion.1
  267.1 3.9 reverse_select_fusion.1
  271.0 1.6 collective-permute-start.4
  272.6 1.0 fusion.69
  273.6 2.0 copy.33
  275.6 2.1 copy.30
  277.7 0.2 fusion.57
  277.9 0.6 compare_reduce_fusion
  278.6 0.1 convert_reduce_fusion
  278.7 0.2 fusion.48
  278.9 4.5 %fusion.14 = bf16[8,2048]{1,0:T(8,128)(2,1)S(1)} fusion(bf16[1600,2048]{1,0:T(8,128)(2,1)} %param.18, bf16[1,8,2048]{2,1,0:T(8,128)(2,1)S(1)} %copy-done.7, pred[]{:T(512)} %compare_reduce_fusion, bf16[1,8,1600]{2,1,0:T(8,128)(2,1)S(1)} %copy-done.6, f32[8]{0:T(128)S(1)} %add_sqrt_fusion.1, f32[8]{0:T(128)S(1)} %broadcast_multiply_fusion.1), kind=kOutput, calls=%fused_computation.27 | convolution fusion | flops 52512768 | bytes 6644801 | tf_op jit(solution)/shard_map/dot_general | solution.py:100
  283.5 21.0 %all_gather.6 = bf16[128,2048]{1,0:T(8,128)(2,1)S(1)} all-gather(bf16[8,2048]{1,0:T(8,128)(2,1)S(1)} %fusion.14), channel_id=1, replica_groups=mesh['group'=2,'dev'=16] {'dev'}, dimensions={0}, use_global_device_ids=true | all-gather | bytes 557056 | tf_op jit(solution)/shard_map/all_gather | solution.py:106
  304.5 0.7 fusion.70
  305.2 1.8 copy.29
  307.0 2.0 copy.34
  309.1 0.8 copy.31
  309.9 0.1 select_reduce_fusion
  310.0 0.6 fusion.58
  310.6 0.6 iota_compare_fusion.2
  311.3 0.1 fusion.44
  311.4 1.6 bitcast_reduce_fusion
  313.0 2.0 fusion.8
  315.1 0.4 fusion.24
  315.5 1.0 fusion.9
  316.5 1.1 fusion.26
  317.7 0.6 fusion.33
  318.3 0.5 copy-done.8
  318.8 1.1 fusion.71
  319.9 0.3 multiply_reduce_fusion
  320.1 89.6 %collective-permute-done.4 = bf16[16,120,1600]{2,1,0:T(8,128)(2,1)} collective-permute-done((bf16[16,120,1600]{2,1,0:T(8,128)(2,1)}, bf16[16,120,1600]{2,1,0:T(8,128)(2,1)}, u32[]{:S(2)}, u32[]{:S(2)}) %collective-permute-start.4) | collective-permute-done | bytes 6144032 | tf_op jit(solution)/shard_map/ppermute | solution.py:24
  409.7 6.3 %pad_maximum_fusion = bf16[2,16,120,1600]{3,2,1,0:T(8,128)(2,1)S(1)} fusion(bf16[1,16,120,1600]{3,2,1,0:T(8,128)(2,1)} %bitcast.35, bf16[1,16,120,1600]{3,2,1,0:T(8,128)(2,1)} %bitcast.33), kind=kLoop, calls=%fused_computation.1 | loop fusion | flops 6144000 | bytes 24576000 | tf_op jit(solution)/shard_map/stack | solution.py:25
  416.1 6.3 %reverse_select_fusion = bf16[2,16,120,1600]{3,2,1,0:T(8,128)(2,1)} fusion(bf16[2,16,120,1600]{3,2,1,0:T(8,128)(2,1)S(1)} %pad_maximum_fusion, pred[]{:T(512)S(6)} %eq.69), kind=kLoop, calls=%fused_computation | loop fusion | flops 6144000 | bytes 24576000 | tf_op jit(solution)/shard_map/jit(_where)/select_n | solution.py:27
  422.4 19.0 %fusion.13 = bf16[1,256,1600]{1,2,0:T(8,128)(2,1)} fusion(f32[256,1600]{0,1:T(8,128)} %copy-done.2, bf16[3840,1600]{1,0:T(8,128)(2,1)} %bitcast.105, bf16[1600,3840]{0,1:T(8,128)(2,1)} %all-gather.2.cloned.1.call-done, f32[256]{0:T(256)S(1)} %add_sqrt_fusion, f32[256]{0:T(256)S(1)} %broadcast_multiply_fusion, pred[256]{0:T(512)(128)(4,1)S(1)} %iota_compare_fusion.2), kind=kOutput, calls=%fused_computation.24 | convolution fusion | flops 6302760960 | bytes 27035904 | tf_op jit(solution)/shard_map/dot_general | solution.py:138
  (33 shorter events, 0.1 us)
Async XLA Ops:
  6.5 311.7 %copy-start = (bf16[1024,1600]{0,1:T(8,128)(2,1)S(1)}, bf16[1024,1600]{0,1:T(8,128)(2,1)}, u32[]{:S(2)}) copy-start(bf16[1024,1600]{0,1:T(8,128)(2,1)} %param.19) | copy-start | bytes 9830404
  6.5 415.9 %all-gather.2.cloned.1.call-start = ((), (), s32[]{:S(2)}) async-start(), calls=%async_computation | async-start | bytes 13178880 | tf_op jit(solution)/shard_map/all_gather | solution.py:133
  7.3 2.2 collective-permute-start
  12.1 24.2 %collective-permute-start.1 = (bf16[2,120,1600]{2,1,0:T(8,128)(2,1)}, bf16[2,120,1600]{2,1,0:T(8,128)(2,1)}, u32[]{:S(2)}, u32[]{:S(2)}) collective-permute-start(bf16[2,120,1600]{2,1,0:T(8,128)(2,1)} %get-tuple-element.10), channel_id=1, source_target_pairs={{0,2},{1,3},{2,0},{3,1},{4,6},{5,7},{6,4},{7,5},{8,10},{9,11},{10,... | collective-permute-start | bytes 2304008 | tf_op jit(solution)/shard_map/ppermute | solution.py:24
  39.2 71.5 %collective-permute-start.2 = (bf16[4,120,1600]{2,1,0:T(8,128)(2,1)}, bf16[4,120,1600]{2,1,0:T(8,128)(2,1)}, u32[]{:S(2)}, u32[]{:S(2)}) collective-permute-start(bf16[4,120,1600]{2,1,0:T(8,128)(2,1)} %bitcast.28), channel_id=1, source_target_pairs={{0,4},{1,5},{2,6},{3,7},{4,0},{5,1},{6,2},{7,3},{8,12},{9,13},{10,... | collective-permute-start | bytes 4608008 | tf_op jit(solution)/shard_map/ppermute | solution.py:24
  115.2 148.3 %collective-permute-start.3 = (bf16[8,120,1600]{2,1,0:T(8,128)(2,1)}, bf16[8,120,1600]{2,1,0:T(8,128)(2,1)}, u32[]{:S(2)}, u32[]{:S(2)}) collective-permute-start(bf16[8,120,1600]{2,1,0:T(8,128)(2,1)} %bitcast.31), channel_id=1, source_target_pairs={{0,8},{1,9},{2,10},{3,11},{4,12},{5,13},{6,14},{7,15},{8,0},{9,1},... | collective-permute-start | bytes 9216008 | tf_op jit(solution)/shard_map/ppermute | solution.py:24
  267.1 5.5 %copy-start.3 = (bf16[1,256,2048]{2,1,0:T(8,128)(2,1)S(1)}, bf16[1,256,2048]{2,1,0:T(8,128)(2,1)}, u32[]{:S(2)}) copy-start(bf16[1,256,2048]{2,1,0:T(8,128)(2,1)} %param.15) | copy-start | bytes 3145732
  271.0 6.8 %copy-start.9 = (s32[1,16]{1,0:T(1,128)S(1)}, s32[1,16]{1,0:T(1,128)}, u32[]{:S(2)}) copy-start(s32[1,16]{1,0:T(1,128)} %param.24) | copy-start | bytes 196
  271.0 6.8 %copy-start.10 = (s32[1,2]{1,0:T(1,128)S(1)}, s32[1,2]{1,0:T(1,128)}, u32[]{:S(2)}) copy-start(s32[1,2]{1,0:T(1,128)} %param.25) | copy-start | bytes 28
  271.0 7.6 %copy-start.6 = (bf16[1,8,1600]{2,1,0:T(8,128)(2,1)S(1)}, bf16[1,8,1600]{2,1,0:T(8,128)(2,1)}, u32[]{:S(2)}) copy-start(bf16[1,8,1600]{2,1,0:T(8,128)(2,1)} %param.17) | copy-start | bytes 76804
  271.0 7.9 %copy-start.7 = (bf16[1,8,2048]{2,1,0:T(8,128)(2,1)S(1)}, bf16[1,8,2048]{2,1,0:T(8,128)(2,1)}, u32[]{:S(2)}) copy-start(bf16[1,8,2048]{2,1,0:T(8,128)(2,1)} %param.16) | copy-start | bytes 98308
  271.0 138.8 %collective-permute-start.4 = (bf16[16,120,1600]{2,1,0:T(8,128)(2,1)}, bf16[16,120,1600]{2,1,0:T(8,128)(2,1)}, u32[]{:S(2)}, u32[]{:S(2)}) collective-permute-start(bf16[16,120,1600]{2,1,0:T(8,128)(2,1)} %bitcast.34), channel_id=1, source_target_pairs={{0,16},{1,17},{2,18},{3,19},{4,20},{5,21},{6,22},{7,23},{8,24},{9,... | collective-permute-start | bytes 18432008 | tf_op jit(solution)/shard_map/ppermute | solution.py:24
  278.9 31.0 %copy-start.11 = (s32[1,16]{1,0:T(1,128)S(1)}, s32[1,16]{1,0:T(1,128)}, u32[]{:S(2)}) copy-start(s32[1,16]{1,0:T(1,128)} %param.22) | copy-start | bytes 196
  278.9 31.0 %copy-start.12 = (s32[1,16]{1,0:T(1,128)S(1)}, s32[1,16]{1,0:T(1,128)}, u32[]{:S(2)}) copy-start(s32[1,16]{1,0:T(1,128)} %param.23) | copy-start | bytes 196
  315.1 1.4 copy-start.4
  316.5 1.1 copy-start.5
  317.6 1.2 copy-start.8
  319.9 89.9 %copy-start.2 = (f32[256,1600]{0,1:T(8,128)}, f32[256,1600]{0,1:T(8,128)S(1)}, u32[]{:S(2)}) copy-start(f32[256,1600]{0,1:T(8,128)S(1)} %get-tuple-element.21) | copy-start | bytes 4915204
  422.4 19.0 %copy-start.1 = (bf16[1024,1600]{0,1:T(8,128)(2,1)S(1)}, bf16[1024,1600]{0,1:T(8,128)(2,1)}, u32[]{:S(2)}) copy-start(bf16[1024,1600]{0,1:T(8,128)(2,1)} %param.19) | copy-start | bytes 9830404
Sparse Core Ops, SparseCore 0:
  10.2 192.7 all-gather.1
